TPU v7x, 32 devices: a whole 2x2x4 slice. The times are simulated.
32 devices in a mesh: parts: 2 (over y), ctx: 8 (over z, x), tp: 2 (over core).
Axes of the slice: x: 2, y: 2, z: 4, core: 2. Of those that a mesh axis runs over, the one named last changes fastest.
Arguments:
- queries: bfloat16 [2048, 8192], P(('parts', 'ctx'), 'tp'), parts along dimension 0, may hold values from -9 to 9
- episode_key_cache: bfloat16 [128, 16, 1024], P(None, ('parts', 'ctx'), 'tp'), parts along dimension 1, may hold values from -9 to 9
- episode_value_cache: bfloat16 [128, 16, 1024], P(None, ('parts', 'ctx'), 'tp'), parts along dimension 1, may hold values from -6 to 6
- output_gradient: bfloat16 [2048, 8192], P(('parts', 'ctx'), 'tp'), parts along dimension 0, may hold values from -6 to 6
- block_lists: int32 [16, 2], P(('parts', 'ctx')), parts along dimension 0, may hold values from 0 to 7, as said below
- block_counts: int32 [16], P(('parts', 'ctx')), parts along dimension 0, may hold values from 1 to 2
Outputs:
- attn_out: bfloat16 [2048, 8192], P(('parts', 'ctx'), 'tp'), parts along dimension 0
- query_grad: bfloat16 [2048, 8192], P(('parts', 'ctx'), 'tp'), parts along dimension 0
- key_cache_gradient: bfloat16 [128, 16, 1024], P(None, ('parts', 'ctx'), 'tp'), parts along dimension 1
- value_cache_gradient: bfloat16 [128, 16, 1024], P(None, ('parts', 'ctx'), 'tp'), parts along dimension 1
There are 2 independent parts, one for each index of `parts`. A program takes and returns all parts, laid end to end along the dimension named above; each array names one. Nothing has to cross between parts.
Inputs may be any that keep to these rules, and one draw needn't show every extreme that they name: `block_lists`: each row names 2 different key blocks; a query block reads only its first block_counts entries.
All inputs are finite; a program needn't handle non-finite values.
Results may differ from a plain program's by a relative error of at most 0.0085.
The roundings to bfloat16 on the way count: a program that leaves them out, or rounds other values in their place, can miss the bound.
Values may be sent and summed in bfloat16 or wider, within the bound.
No kernel may reach another device: no remote copies, remote signals or barrier semaphores. Data moves between devices by JAX's collectives and lax.ppermute only.
A program may use at most 64 MiB of HBM per device.

v0:
```python
import jax
import jax.numpy as jnp
from jax import lax
from jax.sharding import PartitionSpec as P

QUERY_HEADS = 64
KEY_VALUE_HEADS = 8
HEAD_SIZE = 128
LIST = 2


def attend_group(query_part, key_part, value_part, grad_part, live_slots):
    score_scale = HEAD_SIZE ** (-0.5)
    scores = score_scale * jnp.einsum(
        "qah,jkh->aqjk", query_part, key_part, preferred_element_type=jnp.float32
    )
    masked = jnp.where(live_slots[None, None, :, None], scores, -jnp.inf)
    row_peak = jnp.max(masked, axis=(2, 3), keepdims=True)
    exponent = jnp.exp(masked - row_peak)
    weights = exponent / jnp.sum(exponent, axis=(2, 3), keepdims=True)
    weights_low = weights.astype(jnp.bfloat16)
    attended = jnp.einsum(
        "aqjk,jkh->qah", weights_low, value_part, preferred_element_type=jnp.float32
    ).astype(jnp.bfloat16)
    attended = lax.optimization_barrier(attended)
    row_delta = jnp.sum(grad_part.astype(jnp.float32) * attended.astype(jnp.float32), axis=2)
    weight_grad = jnp.einsum(
        "qah,jkh->aqjk", grad_part, value_part, preferred_element_type=jnp.float32
    )
    score_grad = (weights * (weight_grad - row_delta.T[:, :, None, None])).astype(jnp.bfloat16)
    query_grad = (
        score_scale
        * jnp.einsum("aqjk,jkh->qah", score_grad, key_part, preferred_element_type=jnp.float32)
    ).astype(jnp.bfloat16)
    key_piece = score_scale * jnp.einsum(
        "aqjk,qah->jkh", score_grad, query_part, preferred_element_type=jnp.float32
    )
    value_piece = jnp.einsum(
        "aqjk,qah->jkh", weights_low, grad_part, preferred_element_type=jnp.float32
    )
    return (attended, query_grad, key_piece, value_piece)


def arrange_rows(arrived):
    row_count, slot_count, peer_count, column_count = arrived.shape
    return jnp.transpose(arrived, (1, 2, 0, 3)).reshape(
        slot_count, peer_count * row_count, column_count
    )


def split_rows(pieces, row_count):
    slot_count, row_total, column_count = pieces.shape
    shaped = pieces.reshape(slot_count, row_total // row_count, row_count, column_count)
    return jnp.transpose(shaped, (2, 0, 1, 3))


def owner_sum(arrived, selector):
    summed = jnp.einsum("rjpc,jpn->rnc", arrived, selector, precision=lax.Precision.HIGHEST)
    return summed.astype(jnp.bfloat16)


def shards(
    queries, episode_key_cache, episode_value_cache, output_gradient, block_lists, block_counts
):
    held_keys, held_values = (
        lax.all_to_all(episode_key_cache, "ctx", split_axis=0, concat_axis=1, tiled=True),
        lax.all_to_all(episode_value_cache, "ctx", split_axis=0, concat_axis=1, tiled=True),
    )
    row_count = held_keys.shape[0]
    block_total = held_keys.shape[1]
    local_groups = held_keys.shape[2] // HEAD_SIZE
    queries_per_group = QUERY_HEADS // KEY_VALUE_HEADS
    query_rows = queries.shape[0]
    listed_all = lax.all_gather(block_lists, "ctx", axis=0, tiled=True)
    wanted = listed_all.T
    live_slots = jnp.arange(LIST, dtype=jnp.int32) < block_counts[0]
    selector = (
        wanted[:, :, None] == jnp.arange(block_total, dtype=jnp.int32)[None, None, :]
    ).astype(jnp.float32)
    picked_keys = jnp.take(held_keys, wanted, axis=1)
    picked_values = jnp.take(held_values, wanted, axis=1)

    def run_group(group_index, key_rows, value_rows):
        first_col = group_index * queries_per_group * HEAD_SIZE
        last_col = first_col + queries_per_group * HEAD_SIZE
        query_part = queries[:, first_col:last_col].reshape(
            query_rows, queries_per_group, HEAD_SIZE
        )
        grad_part = output_gradient[:, first_col:last_col].reshape(
            query_rows, queries_per_group, HEAD_SIZE
        )
        return attend_group(query_part, key_rows, value_rows, grad_part, live_slots)

    arrived_keys, arrived_values = (
        lax.all_to_all(picked_keys, "ctx", split_axis=2, concat_axis=2, tiled=True),
        lax.all_to_all(picked_values, "ctx", split_axis=2, concat_axis=2, tiled=True),
    )
    fetched_keys = arrange_rows(arrived_keys)
    fetched_values = arrange_rows(arrived_values)
    results = [
        run_group(
            group_index,
            fetched_keys[:, :, group_index * HEAD_SIZE : (group_index + 1) * HEAD_SIZE],
            fetched_values[:, :, group_index * HEAD_SIZE : (group_index + 1) * HEAD_SIZE],
        )
        for group_index in range(local_groups)
    ]
    key_pieces = jnp.concatenate([outcome[2] for outcome in results], axis=2)
    value_pieces = jnp.concatenate([outcome[3] for outcome in results], axis=2)
    back_keys, back_values = (
        lax.all_to_all(
            split_rows(key_pieces, row_count).astype(jnp.bfloat16),
            "ctx",
            split_axis=2,
            concat_axis=2,
            tiled=True,
        ).astype(jnp.float32),
        lax.all_to_all(
            split_rows(value_pieces, row_count).astype(jnp.bfloat16),
            "ctx",
            split_axis=2,
            concat_axis=2,
            tiled=True,
        ).astype(jnp.float32),
    )
    row_key_grad = owner_sum(back_keys, selector)
    row_value_grad = owner_sum(back_values, selector)
    key_cache_gradient, value_cache_gradient = (
        lax.all_to_all(row_key_grad, "ctx", split_axis=1, concat_axis=0, tiled=True),
        lax.all_to_all(row_value_grad, "ctx", split_axis=1, concat_axis=0, tiled=True),
    )
    attn_out = jnp.concatenate(
        [outcome[0].reshape(query_rows, queries_per_group * HEAD_SIZE) for outcome in results],
        axis=1,
    )
    query_grad = jnp.concatenate(
        [outcome[1].reshape(query_rows, queries_per_group * HEAD_SIZE) for outcome in results],
        axis=1,
    )
    return (attn_out, query_grad, key_cache_gradient, value_cache_gradient)


def solution(mesh):
    placed = (
        P(("parts", "ctx"), "tp"),
        P(None, ("parts", "ctx"), "tp"),
        P(None, ("parts", "ctx"), "tp"),
        P(("parts", "ctx"), "tp"),
        P(("parts", "ctx"), None),
        P(("parts", "ctx")),
    )
    return jax.shard_map(
        shards,
        mesh=mesh,
        in_specs=placed,
        out_specs=(
            P(("parts", "ctx"), "tp"),
            P(("parts", "ctx"), "tp"),
            P(None, ("parts", "ctx"), "tp"),
            P(None, ("parts", "ctx"), "tp"),
        ),
        check_vma=False,
    )
```

profile of v0, /device:TPU:0, one launch (start us, length us, event | category | flops | bytes accessed | tf_op | source)
XLA Modules:
  0.0 133.8 jit_solution(3935929716690283083)
XLA Ops:
  0.6 0.5 broadcast.110
  1.1 1.6 %reduce = bf16[128,512]{1,0:T(8,128)(2,1)S(1)} reduce(bf16[128,1,512]{2,0,1:T(8,128)(2,1)} %param.10, bf16[]{:T(256)} %broadcast.110), dimensions={1}, to_apply=%copy.184.reduce_sub_computation | reduce | bytes 262146 | tf_op args[2]
  2.7 0.7 reshape.189
  3.5 7.3 %all-to-all-start = ((bf16[8,2,4096]{2,1,0:T(2,128)(2,1)}), bf16[8,2,4096]{2,1,0:T(2,128)(2,1)S(1)}, u32[]{:S(2)}, u32[]{:S(2)}) async-start(bf16[8,2,4096]{2,1,0:T(2,128)(2,1)} %reshape.189), calls=%async_computation | async-start | bytes 262144 | tf_op jit(solution)/shard_map/all_to_all | solution.py:67
  10.7 21.1 %all-gather = s32[8,1,2]{2,1,0:T(1,128)S(1)} all-gather(s32[1,1,2]{2,1,0:T(1,128)} %bitcast.467), channel_id=1, replica_groups=mesh['parts'=2,'ctx'=8,'tp'=2] {'ctx'}, dimensions={0}, use_global_device_ids=true | all-gather | bytes 72 | tf_op jit(solution)/shard_map/all_gather | solution.py:74
  32.1 1.6 %reduce.1 = bf16[128,512]{1,0:T(8,128)(2,1)S(1)} reduce(bf16[128,1,512]{2,0,1:T(8,128)(2,1)} %param.9, bf16[]{:T(256)} %broadcast.110), dimensions={1}, to_apply=%copy.188.reduce_sub_computation | reduce | bytes 262146 | tf_op args[1]
  33.6 0.7 reshape.187
  34.4 3.4 %all-to-all-start.2 = ((bf16[8,2,4096]{2,1,0:T(2,128)(2,1)}), bf16[8,2,4096]{2,1,0:T(2,128)(2,1)S(1)}, u32[]{:S(2)}, u32[]{:S(2)}) async-start(bf16[8,2,4096]{2,1,0:T(2,128)(2,1)} %reshape.187), calls=%async_computation.2 | async-start | bytes 262144 | tf_op jit(solution)/shard_map/all_to_all | solution.py:66
  37.9 7.1 %all-to-all-done.2 = bf16[8,2,4096]{2,1,0:T(2,128)(2,1)S(1)} async-done(((bf16[8,2,4096]{2,1,0:T(2,128)(2,1)}), bf16[8,2,4096]{2,1,0:T(2,128)(2,1)S(1)}, u32[]{:S(2)}, u32[]{:S(2)}) %all-to-all-start.2) | async-done | bytes 131104 | tf_op jit(solution)/shard_map/all_to_all | solution.py:66
  45.2 0.6 gather_fusion
  45.8 0.6 gather_fusion.1
  46.5 0.7 copy.189
  47.2 3.4 %all-to-all-start.3 = ((bf16[16,2,8,512]{3,0,1,2:T(8,128)(2,1)}), bf16[16,2,8,512]{3,0,1,2:T(8,128)(2,1)S(1)}, u32[]{:S(2)}, u32[]{:S(2)}) async-start(bf16[16,2,8,512]{3,0,1,2:T(8,128)(2,1)} %copy.189), calls=%async_computation.3 | async-start | bytes 524288 | tf_op jit(solution)/shard_map/all_to_all | solution.py:95
  52.1 0.5 copy-done.9
  52.6 0.9 fusion.71
  53.5 1.2 copy.210
  54.6 0.8 copy.215
  55.9 0.7 copy.185
  56.6 2.2 %all-to-all-done.3 = bf16[16,2,8,512]{3,0,1,2:T(8,128)(2,1)S(1)} async-done(((bf16[16,2,8,512]{3,0,1,2:T(8,128)(2,1)}), bf16[16,2,8,512]{3,0,1,2:T(8,128)(2,1)S(1)}, u32[]{:S(2)}, u32[]{:S(2)}) %all-to-all-start.3) | async-done | bytes 262176 | tf_op jit(solution)/shard_map/all_to_all | solution.py:95
  58.8 4.0 %all-to-all-start.1 = ((bf16[16,2,8,512]{3,0,1,2:T(8,128)(2,1)}), bf16[16,2,8,512]{3,0,1,2:T(8,128)(2,1)}, u32[]{:S(2)}, u32[]{:S(2)}) async-start(bf16[16,2,8,512]{3,0,1,2:T(8,128)(2,1)} %copy.185), calls=%async_computation.1 | async-start | bytes 524288 | tf_op jit(solution)/shard_map/all_to_all | solution.py:96
  64.2 6.8 %all-to-all-done.1 = bf16[16,2,8,512]{3,0,1,2:T(8,128)(2,1)} async-done(((bf16[16,2,8,512]{3,0,1,2:T(8,128)(2,1)}), bf16[16,2,8,512]{3,0,1,2:T(8,128)(2,1)}, u32[]{:S(2)}, u32[]{:S(2)}) %all-to-all-start.1) | async-done | bytes 262176 | tf_op jit(solution)/shard_map/all_to_all | solution.py:96
  71.1 1.0 copy.186
  73.4 1.0 fusion.28
  75.3 0.5 copy-done
  76.8 0.9 fusion.30
  78.7 0.9 fusion.50
  82.2 0.8 copy.238
  83.1 2.0 %copy.239 = bf16[16,2,8,512]{3,1,0,2:T(2,128)(2,1)} copy(bf16[16,2,8,512]{3,0,2,1:T(8,128)(2,1)} %bitcast.447) | data formatting | bytes 524288 | tf_op jit(solution)/shard_map/convert_element_type | solution.py:112
  85.0 4.0 %all-to-all-start.4 = ((bf16[16,2,8,512]{3,1,0,2:T(2,128)(2,1)}), bf16[16,2,8,512]{3,1,0,2:T(2,128)(2,1)}, u32[]{:S(2)}, u32[]{:S(2)}) async-start(bf16[16,2,8,512]{3,1,0,2:T(2,128)(2,1)} %copy.239), calls=%async_computation.4 | async-start | bytes 524288 | tf_op jit(solution)/shard_map/all_to_all | solution.py:111
  89.1 1.0 fusion.29
  90.4 1.1 copy.231
  91.6 1.1 copy.232
  92.7 0.9 copy.208
  93.9 0.9 pad_maximum_fusion.3
  94.9 1.0 copy.247
  95.9 1.5 %all-to-all-done.4 = bf16[16,2,8,512]{3,1,0,2:T(2,128)(2,1)} async-done(((bf16[16,2,8,512]{3,1,0,2:T(2,128)(2,1)}), bf16[16,2,8,512]{3,1,0,2:T(2,128)(2,1)}, u32[]{:S(2)}, u32[]{:S(2)}) %all-to-all-start.4) | async-done | bytes 262176 | tf_op jit(solution)/shard_map/all_to_all | solution.py:111
  97.3 4.4 %all-to-all-start.6 = ((bf16[16,2,8,512]{3,1,0,2:T(2,128)(2,1)}), bf16[16,2,8,512]{3,1,0,2:T(2,128)(2,1)S(1)}, u32[]{:S(2)}, u32[]{:S(2)}) async-start(bf16[16,2,8,512]{3,1,0,2:T(2,128)(2,1)} %copy.247), calls=%async_computation.6 | async-start | bytes 524288 | tf_op jit(solution)/shard_map/all_to_all | solution.py:118
  102.3 1.2 fusion.39
  103.6 0.7 copy.241
  104.3 6.1 %all-to-all-done.6 = bf16[16,2,8,512]{3,1,0,2:T(2,128)(2,1)S(1)} async-done(((bf16[16,2,8,512]{3,1,0,2:T(2,128)(2,1)}), bf16[16,2,8,512]{3,1,0,2:T(2,128)(2,1)S(1)}, u32[]{:S(2)}, u32[]{:S(2)}) %all-to-all-start.6) | async-done | bytes 262176 | tf_op jit(solution)/shard_map/all_to_all | solution.py:118
  110.4 3.8 %all-to-all-start.5 = ((bf16[16,8,512]{2,0,1:T(8,128)(2,1)}), bf16[16,8,512]{2,0,1:T(8,128)(2,1)S(1)}, u32[]{:S(2)}, u32[]{:S(2)}) async-start(bf16[16,8,512]{2,0,1:T(8,128)(2,1)} %copy.241), calls=%async_computation.5 | async-start | bytes 262144 | tf_op jit(solution)/shard_map/all_to_all | solution.py:129
  114.5 0.7 copy.249
  115.2 6.5 %all-to-all-done.5 = bf16[16,8,512]{2,0,1:T(8,128)(2,1)S(1)} async-done(((bf16[16,8,512]{2,0,1:T(8,128)(2,1)}), bf16[16,8,512]{2,0,1:T(8,128)(2,1)S(1)}, u32[]{:S(2)}, u32[]{:S(2)}) %all-to-all-start.5) | async-done | bytes 131104 | tf_op jit(solution)/shard_map/all_to_all | solution.py:129
  121.8 3.4 %all-to-all-start.7 = ((bf16[16,8,512]{2,0,1:T(8,128)(2,1)}), bf16[16,8,512]{2,0,1:T(8,128)(2,1)S(1)}, u32[]{:S(2)}, u32[]{:S(2)}) async-start(bf16[16,8,512]{2,0,1:T(8,128)(2,1)} %copy.249), calls=%async_computation.7 | async-start | bytes 262144 | tf_op jit(solution)/shard_map/all_to_all | solution.py:130
  125.2 1.5 %pad_maximum_fusion = (bf16[128,4096]{1,0:T(8,128)(2,1)}, bf16[128,4096]{1,0:T(8,128)(2,1)}) fusion(bf16[128,1024]{1,0:T(8,128)(2,1)S(1)} %copy.209, bf16[128,1024]{1,0:T(8,128)(2,1)S(1)} %copy-done.7, bf16[128,1024]{1,0:T(8,128)(2,1)S(1)} %copy.207, bf16[128,1024]{1,0:T(8,128)(2,1)S(1)} %copy.206, bf16[128,1024]{1,0:T(8,128)(2,1)S(1)} %copy.233, ...), kind=kLoop, calls=%fused_computation.80 | loop fusion | flops 8388608 | bytes 4194304 | tf_op jit(solution)/shard_map/concatenate | solution.py:132
  126.7 5.8 %all-to-all-done.7 = bf16[16,8,512]{2,0,1:T(8,128)(2,1)S(1)} async-done(((bf16[16,8,512]{2,0,1:T(8,128)(2,1)}), bf16[16,8,512]{2,0,1:T(8,128)(2,1)S(1)}, u32[]{:S(2)}, u32[]{:S(2)}) %all-to-all-start.7) | async-done | bytes 131104 | tf_op jit(solution)/shard_map/all_to_all | solution.py:130
  132.4 0.7 copy.351
  133.1 0.7 copy.352
  (82 shorter events, 11.3 us)
Async XLA Ops:
  3.5 30.9 %all-to-all-start = ((bf16[8,2,4096]{2,1,0:T(2,128)(2,1)}), bf16[8,2,4096]{2,1,0:T(2,128)(2,1)S(1)}, u32[]{:S(2)}, u32[]{:S(2)}) async-start(bf16[8,2,4096]{2,1,0:T(2,128)(2,1)} %reshape.189), calls=%async_computation | async-start | bytes 262144 | tf_op jit(solution)/shard_map/all_to_all | solution.py:67
  34.4 10.7 %all-to-all-start.2 = ((bf16[8,2,4096]{2,1,0:T(2,128)(2,1)}), bf16[8,2,4096]{2,1,0:T(2,128)(2,1)S(1)}, u32[]{:S(2)}, u32[]{:S(2)}) async-start(bf16[8,2,4096]{2,1,0:T(2,128)(2,1)} %reshape.187), calls=%async_computation.2 | async-start | bytes 262144 | tf_op jit(solution)/shard_map/all_to_all | solution.py:66
  46.3 4.3 %copy-start.8 = (bf16[128,4096]{1,0:T(8,128)(2,1)S(1)}, bf16[128,4096]{1,0:T(8,128)(2,1)}, u32[]{:S(2)}) copy-start(bf16[128,4096]{1,0:T(8,128)(2,1)} %param.8) | copy-start | bytes 3145732
  47.2 11.6 %all-to-all-start.3 = ((bf16[16,2,8,512]{3,0,1,2:T(8,128)(2,1)}), bf16[16,2,8,512]{3,0,1,2:T(8,128)(2,1)S(1)}, u32[]{:S(2)}, u32[]{:S(2)}) async-start(bf16[16,2,8,512]{3,0,1,2:T(8,128)(2,1)} %copy.189), calls=%async_computation.3 | async-start | bytes 524288 | tf_op jit(solution)/shard_map/all_to_all | solution.py:95
  51.4 1.2 copy-start.9
  53.5 2.2 %copy-start.11 = (bf16[128,1024]{1,0:T(8,128)(2,1)S(1)}, bf16[128,1024]{1,0:T(8,128)(2,1)}, u32[]{:S(2)}) copy-start(bf16[128,1024]{1,0:T(8,128)(2,1)} %get-tuple-element.8) | copy-start | bytes 786436
  55.7 8.3 %copy-start.1 = (bf16[128,1024]{0,1:T(8,128)(2,1)}, bf16[128,1024]{0,1:T(8,128)(2,1)S(1)}, u32[]{:S(2)}) copy-start(bf16[128,1024]{0,1:T(8,128)(2,1)S(1)} %copy.225) | copy-start | bytes 786436
  58.8 12.3 %all-to-all-start.1 = ((bf16[16,2,8,512]{3,0,1,2:T(8,128)(2,1)}), bf16[16,2,8,512]{3,0,1,2:T(8,128)(2,1)}, u32[]{:S(2)}, u32[]{:S(2)}) async-start(bf16[16,2,8,512]{3,0,1,2:T(8,128)(2,1)} %copy.185), calls=%async_computation.1 | async-start | bytes 524288 | tf_op jit(solution)/shard_map/all_to_all | solution.py:96
  62.8 0.7 copy-start.3
  71.1 1.3 copy-start.2
  72.4 1.0 copy-start.4
  74.8 1.0 copy-start
  80.0 0.8 copy-start.5
  82.2 6.9 %copy-start.6 = (bf16[8,128,2,128]{1,3,0,2:T(8,128)(2,1)S(1)}, bf16[8,128,2,128]{1,3,0,2:T(8,128)(2,1)}, u32[]{:S(2)}) copy-start(bf16[8,128,2,128]{1,3,0,2:T(8,128)(2,1)} %copy-done.5) | copy-start | bytes 1572868
  83.1 7.0 %copy-start.10 = (bf16[128,8,128]{2,0,1:T(8,128)(2,1)S(1)}, bf16[128,8,128]{2,0,1:T(8,128)(2,1)}, u32[]{:S(2)}) copy-start(bf16[128,8,128]{2,0,1:T(8,128)(2,1)} %fusion.28) | copy-start | bytes 786436
  85.0 12.3 %all-to-all-start.4 = ((bf16[16,2,8,512]{3,1,0,2:T(2,128)(2,1)}), bf16[16,2,8,512]{3,1,0,2:T(2,128)(2,1)}, u32[]{:S(2)}, u32[]{:S(2)}) async-start(bf16[16,2,8,512]{3,1,0,2:T(2,128)(2,1)} %copy.239), calls=%async_computation.4 | async-start | bytes 524288 | tf_op jit(solution)/shard_map/all_to_all | solution.py:111
  97.3 13.1 %all-to-all-start.6 = ((bf16[16,2,8,512]{3,1,0,2:T(2,128)(2,1)}), bf16[16,2,8,512]{3,1,0,2:T(2,128)(2,1)S(1)}, u32[]{:S(2)}, u32[]{:S(2)}) async-start(bf16[16,2,8,512]{3,1,0,2:T(2,128)(2,1)} %copy.247), calls=%async_computation.6 | async-start | bytes 524288 | tf_op jit(solution)/shard_map/all_to_all | solution.py:118
  102.3 22.8 %copy-start.7 = (bf16[128,1024]{1,0:T(8,128)(2,1)S(1)}, bf16[128,1024]{1,0:T(8,128)(2,1)}, u32[]{:S(2)}) copy-start(bf16[128,1024]{1,0:T(8,128)(2,1)} %copy.208) | copy-start | bytes 786436
  110.4 11.3 %all-to-all-start.5 = ((bf16[16,8,512]{2,0,1:T(8,128)(2,1)}), bf16[16,8,512]{2,0,1:T(8,128)(2,1)S(1)}, u32[]{:S(2)}, u32[]{:S(2)}) async-start(bf16[16,8,512]{2,0,1:T(8,128)(2,1)} %copy.241), calls=%async_computation.5 | async-start | bytes 262144 | tf_op jit(solution)/shard_map/all_to_all | solution.py:129
  121.8 10.7 %all-to-all-start.7 = ((bf16[16,8,512]{2,0,1:T(8,128)(2,1)}), bf16[16,8,512]{2,0,1:T(8,128)(2,1)S(1)}, u32[]{:S(2)}, u32[]{:S(2)}) async-start(bf16[16,8,512]{2,0,1:T(8,128)(2,1)} %copy.249), calls=%async_computation.7 | async-start | bytes 262144 | tf_op jit(solution)/shard_map/all_to_all | solution.py:130
where the time goes:
time: 135 us; the launch traced here: 134 us
  waiting for transfers between devices  36 us (27%)
  starting transfers between devices  33.8 us (25%)
  local copies, waits for them, and re-layouts  22.3 us (17%)
  blocking collectives  21.1 us (16%)
  matrix products  11.2 us (8%)
  other arithmetic  7.34 us (5%)
  between operations  1.9 us (1%)
    all_gather x1, blocking collectives, shards(): listed_all = lax.all_gather(block_lists, 'ctx', axis=0, tiled=True)  21.1 us
    all_to_all x1, starting transfers between devices, shards(): lax.all_to_all(episode_value_cache, 'ctx', split_axis=0, concat_axis=1, t...  7.28 us
    all_to_all x1, waiting for transfers between devices, shards(): lax.all_to_all(episode_key_cache, 'ctx', split_axis=0, concat_axis=1, til...  7.1 us
    all_to_all x1, waiting for transfers between devices, shards(): lax.all_to_all(picked_values, 'ctx', split_axis=2, concat_axis=2, tiled=T...  6.83 us
    all_to_all x1, waiting for transfers between devices, shards(): lax.all_to_all(row_key_grad, 'ctx', split_axis=1, concat_axis=0, tiled=True)  6.53 us
    unnamed x37, local copies, waits for them, and re-layouts  6.16 us
    all_to_all x1, waiting for transfers between devices, shards(): lax.all_to_all(split_rows(value_pieces, row_count).astype(jnp.bfloat16),...  6.15 us
    all_to_all x1, waiting for transfers between devices, shards(): lax.all_to_all(row_value_grad, 'ctx', split_axis=1, concat_axis=0, tiled=...  5.78 us
  transfers between devices with their start and end apart: 8, of which 7 were waited for; matrix products, arithmetic and copies ran while one was open for 15% of the time, Pallas kernels for 0%

commit v1 on v0

--- a/solution.py
+++ b/solution.py
@@ -63,7 +63,12 @@
     queries, episode_key_cache, episode_value_cache, output_gradient, block_lists, block_counts
 ):
     held_keys, held_values = (
-        lax.all_to_all(episode_key_cache, "ctx", split_axis=0, concat_axis=1, tiled=True),
+        jnp.concatenate(
+            lax.all_to_all(
+                jnp.stack(jnp.split(episode_key_cache, lax.axis_size("ctx"), axis=0)), "ctx", 0, 0
+            ),
+            axis=1,
+        ),
         lax.all_to_all(episode_value_cache, "ctx", split_axis=0, concat_axis=1, tiled=True),
     )
     row_count = held_keys.shape[0]

time: 135 us -> 143 us (1.059)
  local copies, waits for them, and re-layouts: 22.3 us -> 32 us
  other arithmetic: 7.34 us -> 5.75 us
    unnamed x37 -> x41, local copies, waits for them, and re-layouts: 6.16 us -> 14.5 us
    unnamed x2 -> x1, other arithmetic: 3.16 us -> 1.58 us
  transfers between devices with their start and end apart: 8 -> 8, of which waited for: 7 -> 7; matrix products, arithmetic and copies ran while one was open for 15% -> 20% of each run, Pallas kernels for 0% -> 0%
where the time goes in v1:
time: 143 us; the launch traced here: 141 us
  waiting for transfers between devices  35.5 us (25%)
  starting transfers between devices  33.8 us (24%)
  local copies, waits for them, and re-layouts  32 us (22%)
  blocking collectives  21.1 us (15%)
  matrix products  11.2 us (8%)
  other arithmetic  5.75 us (4%)
  between operations  1.89 us (1%)
    all_gather x1, blocking collectives, shards(): listed_all = lax.all_gather(block_lists, 'ctx', axis=0, tiled=True)  21.1 us
    unnamed x41, local copies, waits for them, and re-layouts  14.5 us
    all_to_all x1, starting transfers between devices, shards(): lax.all_to_all(episode_value_cache, 'ctx', split_axis=0, concat_axis=1, t...  7.28 us
    all_to_all x1, waiting for transfers between devices, shards(): lax.all_to_all(picked_values, 'ctx', split_axis=2, concat_axis=2, tiled=T...  6.83 us
    all_to_all x1, waiting for transfers between devices, shards(): lax.all_to_all(row_key_grad, 'ctx', split_axis=1, concat_axis=0, tiled=True)  6.53 us
    all_to_all x1, waiting for transfers between devices, shards(): lax.all_to_all(jnp.stack(jnp.split(episode_key_cache, lax.axis_size('ctx'...  6.52 us
    all_to_all x1, waiting for transfers between devices, shards(): lax.all_to_all(split_rows(value_pieces, row_count).astype(jnp.bfloat16),...  6.15 us
    all_to_all x1, waiting for transfers between devices, shards(): lax.all_to_all(row_value_grad, 'ctx', split_axis=1, concat_axis=0, tiled=...  5.78 us
  transfers between devices with their start and end apart: 8, of which 7 were waited for; matrix products, arithmetic and copies ran while one was open for 20% of the time, Pallas kernels for 0%

profile of v1, /device:TPU:0, one launch (start us, length us, event | category | flops | bytes accessed | tf_op | source)
XLA Modules:
  0.0 141.3 jit_solution(12382182508718753458)
XLA Ops:
  1.1 1.6 %reduce = bf16[128,512]{1,0:T(8,128)(2,1)S(1)} reduce(bf16[128,1,512]{2,0,1:T(8,128)(2,1)} %param.10, bf16[]{:T(256)} %broadcast.110), dimensions={1}, to_apply=%copy.183.reduce_sub_computation | reduce | bytes 262146 | tf_op args[2]
  2.7 0.7 reshape.195
  3.5 7.3 %all-to-all-start = ((bf16[8,2,4096]{2,1,0:T(2,128)(2,1)}), bf16[8,2,4096]{2,1,0:T(2,128)(2,1)S(1)}, u32[]{:S(2)}, u32[]{:S(2)}) async-start(bf16[8,2,4096]{2,1,0:T(2,128)(2,1)} %reshape.195), calls=%async_computation | async-start | bytes 262144 | tf_op jit(solution)/shard_map/all_to_all | solution.py:72
  10.7 21.1 %all-gather = s32[8,1,2]{2,1,0:T(1,128)S(1)} all-gather(s32[1,1,2]{2,1,0:T(1,128)} %bitcast.481), channel_id=1, replica_groups=mesh['parts'=2,'ctx'=8,'tp'=2] {'ctx'}, dimensions={0}, use_global_device_ids=true | all-gather | bytes 72 | tf_op jit(solution)/shard_map/all_gather | solution.py:79
  32.0 1.3 constant_dynamic-update-slice_fusion.7
  33.3 1.3 constant_dynamic-update-slice_fusion.6
  34.6 1.3 constant_dynamic-update-slice_fusion.5
  35.9 1.3 constant_dynamic-update-slice_fusion.4
  37.3 1.3 constant_dynamic-update-slice_fusion.3
  38.6 1.3 constant_dynamic-update-slice_fusion.2
  39.9 1.3 constant_dynamic-update-slice_fusion.1
  41.3 1.3 constant_dynamic-update-slice_fusion
  42.6 3.4 %all-to-all-start.2 = ((bf16[8,16,1,512]{3,1,2,0:T(8,128)(2,1)}), bf16[8,16,1,512]{3,1,2,0:T(8,128)(2,1)S(1)}, u32[]{:S(2)}, u32[]{:S(2)}) async-start(bf16[8,16,1,512]{3,1,2,0:T(8,128)(2,1)} %constant_dynamic-update-slice_fusion), calls=%async_computation.2 | async-start | bytes 262144 | tf_op jit(solution)/shard_map/all_to_all | solution.py:67
  46.8 6.5 %all-to-all-done.2 = bf16[8,16,1,512]{3,1,2,0:T(8,128)(2,1)S(1)} async-done(((bf16[8,16,1,512]{3,1,2,0:T(8,128)(2,1)}), bf16[8,16,1,512]{3,1,2,0:T(8,128)(2,1)S(1)}, u32[]{:S(2)}, u32[]{:S(2)}) %all-to-all-start.2) | async-done | bytes 131104 | tf_op jit(solution)/shard_map/all_to_all | solution.py:67
  54.0 0.7 copy.187
  54.7 3.4 %all-to-all-start.3 = ((bf16[16,2,8,512]{3,0,1,2:T(8,128)(2,1)}), bf16[16,2,8,512]{3,0,1,2:T(8,128)(2,1)S(1)}, u32[]{:S(2)}, u32[]{:S(2)}) async-start(bf16[16,2,8,512]{3,0,1,2:T(8,128)(2,1)} %copy.187), calls=%async_computation.3 | async-start | bytes 524288 | tf_op jit(solution)/shard_map/all_to_all | solution.py:100
  60.1 0.9 fusion.71
  61.0 1.2 copy.208
  62.2 0.8 copy.213
  63.4 0.7 copy.184
  64.1 2.2 %all-to-all-done.3 = bf16[16,2,8,512]{3,0,1,2:T(8,128)(2,1)S(1)} async-done(((bf16[16,2,8,512]{3,0,1,2:T(8,128)(2,1)}), bf16[16,2,8,512]{3,0,1,2:T(8,128)(2,1)S(1)}, u32[]{:S(2)}, u32[]{:S(2)}) %all-to-all-start.3) | async-done | bytes 262176 | tf_op jit(solution)/shard_map/all_to_all | solution.py:100
  66.3 4.0 %all-to-all-start.1 = ((bf16[16,2,8,512]{3,0,1,2:T(8,128)(2,1)}), bf16[16,2,8,512]{3,0,1,2:T(8,128)(2,1)}, u32[]{:S(2)}, u32[]{:S(2)}) async-start(bf16[16,2,8,512]{3,0,1,2:T(8,128)(2,1)} %copy.184), calls=%async_computation.1 | async-start | bytes 524288 | tf_op jit(solution)/shard_map/all_to_all | solution.py:101
  71.8 6.8 %all-to-all-done.1 = bf16[16,2,8,512]{3,0,1,2:T(8,128)(2,1)} async-done(((bf16[16,2,8,512]{3,0,1,2:T(8,128)(2,1)}), bf16[16,2,8,512]{3,0,1,2:T(8,128)(2,1)}, u32[]{:S(2)}, u32[]{:S(2)}) %all-to-all-start.1) | async-done | bytes 262176 | tf_op jit(solution)/shard_map/all_to_all | solution.py:101
  78.6 1.0 copy.185
  80.9 1.0 fusion.28
  84.4 0.9 fusion.30
  86.2 0.9 fusion.50
  89.8 0.8 copy.236
  90.6 2.0 %copy.237 = bf16[16,2,8,512]{3,1,0,2:T(2,128)(2,1)} copy(bf16[16,2,8,512]{3,0,2,1:T(8,128)(2,1)} %bitcast.461) | data formatting | bytes 524288 | tf_op jit(solution)/shard_map/convert_element_type | solution.py:117
  92.6 4.0 %all-to-all-start.4 = ((bf16[16,2,8,512]{3,1,0,2:T(2,128)(2,1)}), bf16[16,2,8,512]{3,1,0,2:T(2,128)(2,1)}, u32[]{:S(2)}, u32[]{:S(2)}) async-start(bf16[16,2,8,512]{3,1,0,2:T(2,128)(2,1)} %copy.237), calls=%async_computation.4 | async-start | bytes 524288 | tf_op jit(solution)/shard_map/all_to_all | solution.py:116
  96.6 1.0 fusion.29
  97.9 1.1 copy.229
  99.1 1.1 copy.230
  100.2 0.9 copy.206
  101.4 0.9 pad_maximum_fusion.3
  102.4 1.0 copy.245
  103.4 1.5 %all-to-all-done.4 = bf16[16,2,8,512]{3,1,0,2:T(2,128)(2,1)} async-done(((bf16[16,2,8,512]{3,1,0,2:T(2,128)(2,1)}), bf16[16,2,8,512]{3,1,0,2:T(2,128)(2,1)}, u32[]{:S(2)}, u32[]{:S(2)}) %all-to-all-start.4) | async-done | bytes 262176 | tf_op jit(solution)/shard_map/all_to_all | solution.py:116
  104.9 4.4 %all-to-all-start.6 = ((bf16[16,2,8,512]{3,1,0,2:T(2,128)(2,1)}), bf16[16,2,8,512]{3,1,0,2:T(2,128)(2,1)S(1)}, u32[]{:S(2)}, u32[]{:S(2)}) async-start(bf16[16,2,8,512]{3,1,0,2:T(2,128)(2,1)} %copy.245), calls=%async_computation.6 | async-start | bytes 524288 | tf_op jit(solution)/shard_map/all_to_all | solution.py:123
  109.9 1.2 fusion.39
  111.1 0.7 copy.239
  111.8 6.1 %all-to-all-done.6 = bf16[16,2,8,512]{3,1,0,2:T(2,128)(2,1)S(1)} async-done(((bf16[16,2,8,512]{3,1,0,2:T(2,128)(2,1)}), bf16[16,2,8,512]{3,1,0,2:T(2,128)(2,1)S(1)}, u32[]{:S(2)}, u32[]{:S(2)}) %all-to-all-start.6) | async-done | bytes 262176 | tf_op jit(solution)/shard_map/all_to_all | solution.py:123
  118.0 3.8 %all-to-all-start.5 = ((bf16[16,8,512]{2,0,1:T(8,128)(2,1)}), bf16[16,8,512]{2,0,1:T(8,128)(2,1)S(1)}, u32[]{:S(2)}, u32[]{:S(2)}) async-start(bf16[16,8,512]{2,0,1:T(8,128)(2,1)} %copy.239), calls=%async_computation.5 | async-start | bytes 262144 | tf_op jit(solution)/shard_map/all_to_all | solution.py:134
  122.1 0.7 copy.247
  122.8 6.5 %all-to-all-done.5 = bf16[16,8,512]{2,0,1:T(8,128)(2,1)S(1)} async-done(((bf16[16,8,512]{2,0,1:T(8,128)(2,1)}), bf16[16,8,512]{2,0,1:T(8,128)(2,1)S(1)}, u32[]{:S(2)}, u32[]{:S(2)}) %all-to-all-start.5) | async-done | bytes 131104 | tf_op jit(solution)/shard_map/all_to_all | solution.py:134
  129.3 3.4 %all-to-all-start.7 = ((bf16[16,8,512]{2,0,1:T(8,128)(2,1)}), bf16[16,8,512]{2,0,1:T(8,128)(2,1)S(1)}, u32[]{:S(2)}, u32[]{:S(2)}) async-start(bf16[16,8,512]{2,0,1:T(8,128)(2,1)} %copy.247), calls=%async_computation.7 | async-start | bytes 262144 | tf_op jit(solution)/shard_map/all_to_all | solution.py:135
  132.7 1.5 %pad_maximum_fusion = (bf16[128,4096]{1,0:T(8,128)(2,1)}, bf16[128,4096]{1,0:T(8,128)(2,1)}) fusion(bf16[128,1024]{1,0:T(8,128)(2,1)S(1)} %copy.207, bf16[128,1024]{1,0:T(8,128)(2,1)S(1)} %copy-done.7, bf16[128,1024]{1,0:T(8,128)(2,1)S(1)} %copy.205, bf16[128,1024]{1,0:T(8,128)(2,1)S(1)} %copy.204, bf16[128,1024]{1,0:T(8,128)(2,1)S(1)} %copy.231, ...), kind=kLoop, calls=%fused_computation.80 | loop fusion | flops 8388608 | bytes 4194304 | tf_op jit(solution)/shard_map/concatenate | solution.py:137
  134.2 5.8 %all-to-all-done.7 = bf16[16,8,512]{2,0,1:T(8,128)(2,1)S(1)} async-done(((bf16[16,8,512]{2,0,1:T(8,128)(2,1)}), bf16[16,8,512]{2,0,1:T(8,128)(2,1)S(1)}, u32[]{:S(2)}, u32[]{:S(2)}) %all-to-all-start.7) | async-done | bytes 131104 | tf_op jit(solution)/shard_map/all_to_all | solution.py:135
  140.0 0.7 copy.354
  (86 shorter events, 14.5 us)
Async XLA Ops:
  3.5 39.2 %all-to-all-start = ((bf16[8,2,4096]{2,1,0:T(2,128)(2,1)}), bf16[8,2,4096]{2,1,0:T(2,128)(2,1)S(1)}, u32[]{:S(2)}, u32[]{:S(2)}) async-start(bf16[8,2,4096]{2,1,0:T(2,128)(2,1)} %reshape.195), calls=%async_computation | async-start | bytes 262144 | tf_op jit(solution)/shard_map/all_to_all | solution.py:72
  42.6 10.7 %all-to-all-start.2 = ((bf16[8,16,1,512]{3,1,2,0:T(8,128)(2,1)}), bf16[8,16,1,512]{3,1,2,0:T(8,128)(2,1)S(1)}, u32[]{:S(2)}, u32[]{:S(2)}) async-start(bf16[8,16,1,512]{3,1,2,0:T(8,128)(2,1)} %constant_dynamic-update-slice_fusion), calls=%async_computation.2 | async-start | bytes 262144 | tf_op jit(solution)/shard_map/all_to_all | solution.py:67
  53.9 4.3 %copy-start.8 = (bf16[128,4096]{1,0:T(8,128)(2,1)S(1)}, bf16[128,4096]{1,0:T(8,128)(2,1)}, u32[]{:S(2)}) copy-start(bf16[128,4096]{1,0:T(8,128)(2,1)} %param.8) | copy-start | bytes 3145732
  54.7 11.6 %all-to-all-start.3 = ((bf16[16,2,8,512]{3,0,1,2:T(8,128)(2,1)}), bf16[16,2,8,512]{3,0,1,2:T(8,128)(2,1)S(1)}, u32[]{:S(2)}, u32[]{:S(2)}) async-start(bf16[16,2,8,512]{3,0,1,2:T(8,128)(2,1)} %copy.187), calls=%async_computation.3 | async-start | bytes 524288 | tf_op jit(solution)/shard_map/all_to_all | solution.py:100
  58.9 1.2 copy-start.9
  61.0 2.2 %copy-start.11 = (bf16[128,1024]{1,0:T(8,128)(2,1)S(1)}, bf16[128,1024]{1,0:T(8,128)(2,1)}, u32[]{:S(2)}) copy-start(bf16[128,1024]{1,0:T(8,128)(2,1)} %get-tuple-element.8) | copy-start | bytes 786436
  63.2 8.3 %copy-start.1 = (bf16[128,1024]{0,1:T(8,128)(2,1)}, bf16[128,1024]{0,1:T(8,128)(2,1)S(1)}, u32[]{:S(2)}) copy-start(bf16[128,1024]{0,1:T(8,128)(2,1)S(1)} %copy.223) | copy-start | bytes 786436
  66.3 12.3 %all-to-all-start.1 = ((bf16[16,2,8,512]{3,0,1,2:T(8,128)(2,1)}), bf16[16,2,8,512]{3,0,1,2:T(8,128)(2,1)}, u32[]{:S(2)}, u32[]{:S(2)}) async-start(bf16[16,2,8,512]{3,0,1,2:T(8,128)(2,1)} %copy.184), calls=%async_computation.1 | async-start | bytes 524288 | tf_op jit(solution)/shard_map/all_to_all | solution.py:101
  70.4 0.7 copy-start.3
  78.6 1.3 copy-start.2
  80.0 1.0 copy-start.4
  82.3 1.0 copy-start
  87.6 0.8 copy-start.5
  89.7 6.9 %copy-start.6 = (bf16[8,128,2,128]{1,3,0,2:T(8,128)(2,1)S(1)}, bf16[8,128,2,128]{1,3,0,2:T(8,128)(2,1)}, u32[]{:S(2)}) copy-start(bf16[8,128,2,128]{1,3,0,2:T(8,128)(2,1)} %copy-done.5) | copy-start | bytes 1572868
  90.6 7.0 %copy-start.10 = (bf16[128,8,128]{2,0,1:T(8,128)(2,1)S(1)}, bf16[128,8,128]{2,0,1:T(8,128)(2,1)}, u32[]{:S(2)}) copy-start(bf16[128,8,128]{2,0,1:T(8,128)(2,1)} %fusion.28) | copy-start | bytes 786436
  92.6 12.3 %all-to-all-start.4 = ((bf16[16,2,8,512]{3,1,0,2:T(2,128)(2,1)}), bf16[16,2,8,512]{3,1,0,2:T(2,128)(2,1)}, u32[]{:S(2)}, u32[]{:S(2)}) async-start(bf16[16,2,8,512]{3,1,0,2:T(2,128)(2,1)} %copy.237), calls=%async_computation.4 | async-start | bytes 524288 | tf_op jit(solution)/shard_map/all_to_all | solution.py:116
  104.9 13.1 %all-to-all-start.6 = ((bf16[16,2,8,512]{3,1,0,2:T(2,128)(2,1)}), bf16[16,2,8,512]{3,1,0,2:T(2,128)(2,1)S(1)}, u32[]{:S(2)}, u32[]{:S(2)}) async-start(bf16[16,2,8,512]{3,1,0,2:T(2,128)(2,1)} %copy.245), calls=%async_computation.6 | async-start | bytes 524288 | tf_op jit(solution)/shard_map/all_to_all | solution.py:123
  109.9 22.8 %copy-start.7 = (bf16[128,1024]{1,0:T(8,128)(2,1)S(1)}, bf16[128,1024]{1,0:T(8,128)(2,1)}, u32[]{:S(2)}) copy-start(bf16[128,1024]{1,0:T(8,128)(2,1)} %copy.206) | copy-start | bytes 786436
  118.0 11.3 %all-to-all-start.5 = ((bf16[16,8,512]{2,0,1:T(8,128)(2,1)}), bf16[16,8,512]{2,0,1:T(8,128)(2,1)S(1)}, u32[]{:S(2)}, u32[]{:S(2)}) async-start(bf16[16,8,512]{2,0,1:T(8,128)(2,1)} %copy.239), calls=%async_computation.5 | async-start | bytes 262144 | tf_op jit(solution)/shard_map/all_to_all | solution.py:134
  129.3 10.7 %all-to-all-start.7 = ((bf16[16,8,512]{2,0,1:T(8,128)(2,1)}), bf16[16,8,512]{2,0,1:T(8,128)(2,1)S(1)}, u32[]{:S(2)}, u32[]{:S(2)}) async-start(bf16[16,8,512]{2,0,1:T(8,128)(2,1)} %copy.247), calls=%async_computation.7 | async-start | bytes 262144 | tf_op jit(solution)/shard_map/all_to_all | solution.py:135
